TPU v7x, 512 devices: a whole 4x4x16 slice. The times are simulated.
512 devices in a mesh: pipe: 4 (over y), expert: 32 (over z, core), tensor: 4 (over x).
Axes of the slice: x: 4, y: 4, z: 16, core: 2. Of those that a mesh axis runs over, the one named last changes fastest.
Arguments:
- tokens: bfloat16 [512, 6144], P('expert', ('pipe', 'tensor')), may hold values from -6 to 6
- expert_ids: int32 [512, 2], P('expert'), may hold values from 0 to 7, all different within a row; in each aligned block of 16 rows (0 to 15, 16 to 31, ...) at most 5 rows name the same one
- gates: float32 [512, 2], P('expert'), may hold values from 0.2 to 1
- w_gate: bfloat16 [32, 6144, 2048], P('expert', None, ('pipe', 'tensor')), may hold values from -0.078125 to 0.078125
- w_up: bfloat16 [32, 6144, 2048], P('expert', None, ('pipe', 'tensor')), may hold values from -0.078125 to 0.078125
- w_down: bfloat16 [32, 2048, 6144], P('expert', ('pipe', 'tensor')), may hold values from -0.0625 to 0.0625
- d_out: bfloat16 [512, 6144], P('expert', ('pipe', 'tensor')), may hold values from -6 to 6
Outputs:
- moe_out: bfloat16 [512, 6144], P('expert', ('pipe', 'tensor'))
- grad_tokens: bfloat16 [512, 6144], P('expert', ('pipe', 'tensor'))
- grad_gates: float32 [512, 2], P('expert')
Inputs may be any that keep to these rules, and one draw needn't show every extreme that they name: `expert_ids`: each row names 2 different experts. Among the rows of one index of expert (aligned blocks of 16 rows) no expert is named more than 5 times, a bound that some block reaches.
All inputs are finite; a program needn't handle non-finite values.
Results may differ from a plain program's by a relative error of at most 0.017.
Values may be sent and summed in bfloat16 or wider, within the bound.
No kernel may reach another device: no remote copies, remote signals or barrier semaphores. Data moves between devices by JAX's collectives and lax.ppermute only.
A program may use at most 64 MiB of HBM per device.

v0:
```python
import jax
import jax.numpy as jnp
from jax import lax
from jax.sharding import PartitionSpec as P


def per_device(tokens, expert_ids, gates, w_gate, w_up, w_down, d_out):
    tok_rows = tokens.shape[0]
    top = expert_ids.shape[1]
    devices_all = lax.axis_size("expert")
    experts = min(8, devices_all)
    group = devices_all // experts
    capacity = min(
        tok_rows,
        max(2, max(5 * tok_rows * top // (4 * experts), (tok_rows * top + experts - 1) // experts)),
    )
    slots = experts * capacity
    flat_ids = expert_ids.reshape(-1)
    onehot = (flat_ids[:, None] == jnp.arange(experts, dtype=jnp.int32)[None, :]).astype(jnp.int32)
    position = jnp.sum(jnp.cumsum(onehot, axis=0) * onehot, axis=1) - 1
    slot_of = flat_ids * capacity + position
    picks = (jnp.arange(slots, dtype=jnp.int32)[:, None] == slot_of[None, :]).astype(jnp.float32)
    pick_rows = picks.reshape(slots, tok_rows, top)
    select_tok = jnp.sum(pick_rows, axis=2).astype(jnp.bfloat16)
    select_gate = jnp.sum(pick_rows * gates[None, :, :], axis=2)
    whole_x, whole_dy = (
        lax.all_gather(tokens, ("pipe", "tensor"), axis=1, tiled=True),
        lax.all_gather(d_out, ("pipe", "tensor"), axis=1, tiled=True),
    )
    picked = jnp.dot(select_tok, whole_x, preferred_element_type=jnp.float32).astype(jnp.bfloat16)
    send_x = jnp.repeat(picked.reshape(experts, capacity, -1), group, axis=0)
    scaled = jnp.dot(select_gate, whole_dy.astype(jnp.float32), precision=lax.Precision.HIGHEST)
    send_dy = jnp.repeat(scaled.astype(jnp.bfloat16).reshape(experts, capacity, -1), group, axis=0)
    recv_x, recv_dy = (
        lax.all_to_all(send_x, "expert", split_axis=0, concat_axis=0, tiled=True),
        lax.all_to_all(send_dy, "expert", split_axis=0, concat_axis=0, tiled=True),
    )
    rows_x = recv_x.reshape(devices_all * capacity, -1)
    rows_dy = recv_dy.reshape(devices_all * capacity, -1)
    gate_proj = w_gate[0]
    up_proj = w_up[0]
    down_proj = w_down[0]
    contract_last = (((1,), (1,)), ((), ()))
    h_gate = jnp.dot(rows_x, gate_proj, preferred_element_type=jnp.float32)
    h_up = jnp.dot(rows_x, up_proj, preferred_element_type=jnp.float32)
    sig = jax.nn.sigmoid(h_gate)
    hidden = (h_gate * sig * h_up).astype(jnp.bfloat16)
    out_terms = jnp.dot(hidden, down_proj, preferred_element_type=jnp.float32)
    d_hidden = lax.dot_general(
        rows_dy, down_proj, contract_last, preferred_element_type=jnp.float32
    )
    d_gate_h = (d_hidden * h_up * sig * (1.0 + h_gate * (1.0 - sig))).astype(jnp.bfloat16)
    d_up_h = (d_hidden * h_gate * sig).astype(jnp.bfloat16)
    dx_terms = lax.dot_general(
        d_gate_h, gate_proj, contract_last, preferred_element_type=jnp.float32
    )
    dx_terms = dx_terms + lax.dot_general(
        d_up_h, up_proj, contract_last, preferred_element_type=jnp.float32
    )
    out_share, dx_share = (
        lax.psum_scatter(
            out_terms.astype(jnp.bfloat16), ("pipe", "tensor"), scatter_dimension=1, tiled=True
        ).astype(jnp.float32),
        lax.psum_scatter(
            dx_terms.astype(jnp.bfloat16), ("pipe", "tensor"), scatter_dimension=1, tiled=True
        ).astype(jnp.float32),
    )
    out_slot = out_share.reshape(devices_all, capacity, -1)
    dx_slot = dx_share.reshape(devices_all, capacity, -1)
    back_out, back_dx = (
        lax.all_to_all(
            out_slot.astype(jnp.bfloat16), "expert", split_axis=0, concat_axis=0, tiled=True
        ).astype(out_slot.dtype),
        lax.all_to_all(
            dx_slot.astype(jnp.bfloat16), "expert", split_axis=0, concat_axis=0, tiled=True
        ).astype(dx_slot.dtype),
    )
    out_rows = (
        jnp.sum(back_out.reshape(experts, group, capacity, -1), axis=1)
        .astype(jnp.bfloat16)
        .reshape(slots, -1)
    )
    dx_rows = (
        jnp.sum(back_dx.reshape(experts, group, capacity, -1), axis=1)
        .astype(jnp.bfloat16)
        .reshape(slots, -1)
    )
    assign = picks.T.astype(jnp.bfloat16)
    a_out = jnp.dot(assign, out_rows, preferred_element_type=jnp.float32)
    a_dx = jnp.dot(assign, dx_rows, preferred_element_type=jnp.float32)
    a_out = a_out.reshape(tok_rows, top, -1)
    a_dx = a_dx.reshape(tok_rows, top, -1)
    moe_out = jnp.sum(gates[:, :, None] * a_out, axis=1).astype(jnp.bfloat16)
    grad_tokens = jnp.sum(a_dx, axis=1).astype(jnp.bfloat16)
    partial_dots = jnp.sum(d_out.astype(jnp.float32)[:, None, :] * a_out, axis=2)
    grad_gates = lax.psum(partial_dots, ("pipe", "tensor"))
    return (moe_out, grad_tokens, grad_gates)


def solution(mesh):
    return jax.shard_map(
        per_device,
        mesh=mesh,
        in_specs=(
            P("expert", ("pipe", "tensor")),
            P("expert", None),
            P("expert", None),
            P("expert", None, ("pipe", "tensor")),
            P("expert", None, ("pipe", "tensor")),
            P("expert", ("pipe", "tensor"), None),
            P("expert", ("pipe", "tensor")),
        ),
        out_specs=(
            P("expert", ("pipe", "tensor")),
            P("expert", ("pipe", "tensor")),
            P("expert", None),
        ),
        check_vma=False,
    )
```

profile of v0, /device:TPU:32, one launch (start us, length us, event | category | flops | bytes accessed | tf_op | source)
XLA Modules:
  0.0 613.7 jit_solution(9177753172685445268)
XLA Ops:
  9.3 24.0 %all_gather.6 = bf16[16,6144]{1,0:T(8,128)(2,1)S(1)} all-gather(bf16[16,384]{1,0:T(8,128)(2,1)} %param.7), channel_id=1, replica_groups=mesh['pipe'=4,'expert'=32,'tensor'=4] {'pipe','tensor'}, dimensions={1}, use_global_device_ids=true | all-gather | bytes 208896 | tf_op jit(solution)/shard_map/all_gather | solution.py:27
  34.7 2.0 broadcast_in_dim.4
  36.7 15.5 %all-to-all-start = ((bf16[32,5,6144]{2,1,0:T(8,128)(2,1)}), bf16[32,5,6144]{2,1,0:T(8,128)(2,1)}, u32[]{:S(2)}, u32[]{:S(2)}) async-start(bf16[32,5,6144]{2,1,0:T(8,128)(2,1)} %bitcast.42), calls=%async_computation | async-start | bytes 6291456 | tf_op jit(solution)/shard_map/all_to_all | solution.py:35
  52.2 23.1 %all_gather.7 = bf16[16,6144]{1,0:T(8,128)(2,1)S(1)} all-gather(bf16[16,384]{1,0:T(8,128)(2,1)S(1)} %copy-done.5), channel_id=1, replica_groups=mesh['pipe'=4,'expert'=32,'tensor'=4] {'pipe','tensor'}, dimensions={1}, use_global_device_ids=true | all-gather | bytes 208896 | tf_op jit(solution)/shard_map/all_gather | solution.py:28
  76.2 121.3 %all-to-all-done = bf16[32,5,6144]{2,1,0:T(8,128)(2,1)} async-done(((bf16[32,5,6144]{2,1,0:T(8,128)(2,1)}), bf16[32,5,6144]{2,1,0:T(8,128)(2,1)}, u32[]{:S(2)}, u32[]{:S(2)}) %all-to-all-start) | async-done | bytes 1966112 | tf_op jit(solution)/shard_map/all_to_all | solution.py:35
  197.5 2.1 broadcast_in_dim.5
  199.6 4.6 all-to-all-start.2
  204.2 3.0 reshape.130
  207.3 1.3 fusion.9
  208.7 1.3 fusion.5
  210.0 138.4 %all-to-all-done.2 = bf16[32,5,6144]{2,1,0:T(8,128)(2,1)} async-done(((bf16[32,5,6144]{2,1,0:T(8,128)(2,1)}), bf16[32,5,6144]{2,1,0:T(8,128)(2,1)}, u32[]{:S(2)}, u32[]{:S(2)}) %all-to-all-start.2) | async-done | bytes 1966112 | tf_op jit(solution)/shard_map/all_to_all | solution.py:36
  348.3 3.0 reshape.135
  351.4 2.1 fusion.1
  355.6 2.8 copy.34
  358.4 2.2 convolution_convert_fusion
  360.6 2.8 copy.32
  363.4 76.2 %reduce-scatter.9.cloned.1.call-done = bf16[384,160]{1,0:T(8,128)(2,1)} async-done(((bf16[6144,160]{1,0:T(8,128)(2,1)}), bf16[384,160]{1,0:T(8,128)(2,1)}) %reduce-scatter.9.cloned.1.call-update) | async-done | bytes 122896
  439.6 1.1 copy.35
  441.4 12.8 %all-to-all-start.3 = ((bf16[32,5,384]{2,1,0:T(8,128)(2,1)}), bf16[32,5,384]{2,1,0:T(8,128)(2,1)S(1)}, u32[]{:S(2)}, u32[]{:S(2)}) async-start(bf16[32,5,384]{2,1,0:T(8,128)(2,1)} %convert_element_type.142), calls=%async_computation.3 | async-start | bytes 393216 | tf_op jit(solution)/shard_map/all_to_all | solution.py:74
  454.2 80.1 %reduce-scatter.7.cloned.1.call-done = bf16[384,160]{1,0:T(8,128)(2,1)} async-done(((bf16[6144,160]{1,0:T(8,128)(2,1)}), bf16[384,160]{1,0:T(8,128)(2,1)}) %reduce-scatter.7.cloned.1.call-update) | async-done | bytes 122896
  534.3 1.1 copy.33
  536.1 12.8 %all-to-all-start.1 = ((bf16[32,5,384]{2,1,0:T(8,128)(2,1)}), bf16[32,5,384]{2,1,0:T(8,128)(2,1)S(1)}, u32[]{:S(2)}, u32[]{:S(2)}) async-start(bf16[32,5,384]{2,1,0:T(8,128)(2,1)} %convert_element_type.134), calls=%async_computation.1 | async-start | bytes 393216 | tf_op jit(solution)/shard_map/all_to_all | solution.py:71
  549.8 17.5 %all-to-all-done.1 = bf16[32,5,384]{2,1,0:T(8,128)(2,1)S(1)} async-done(((bf16[32,5,384]{2,1,0:T(8,128)(2,1)}), bf16[32,5,384]{2,1,0:T(8,128)(2,1)S(1)}, u32[]{:S(2)}, u32[]{:S(2)}) %all-to-all-start.1) | async-done | bytes 122912 | tf_op jit(solution)/shard_map/all_to_all | solution.py:71
  568.2 38.7 %psum.7 = f32[16,2]{0,1:T(2,128)} all-reduce(f32[16,2]{0,1:T(2,128)S(1)} %get-tuple-element.3), channel_id=1, replica_groups=mesh['pipe'=4,'expert'=32,'tensor'=4] {'pipe','tensor'}, use_global_device_ids=true, to_apply=%region_11.12 | all-reduce | flops 32 | bytes 256 | tf_op jit(solution)/shard_map/psum | solution.py:96
  (44 shorter events, 9.8 us)
Async XLA Ops:
  7.2 200.1 %copy-start = (bf16[1,6144,128]{2,1,0:T(8,128)(2,1)S(1)}, bf16[1,6144,128]{2,1,0:T(8,128)(2,1)}, u32[]{:S(2)}) copy-start(bf16[1,6144,128]{2,1,0:T(8,128)(2,1)} %param.10) | copy-start | bytes 4718596
  36.7 15.5 %copy-start.5 = (bf16[16,384]{1,0:T(8,128)(2,1)S(1)}, bf16[16,384]{1,0:T(8,128)(2,1)}, u32[]{:S(2)}) copy-start(bf16[16,384]{1,0:T(8,128)(2,1)} %param.13) | copy-start | bytes 36868
  36.7 160.8 %all-to-all-start = ((bf16[32,5,6144]{2,1,0:T(8,128)(2,1)}), bf16[32,5,6144]{2,1,0:T(8,128)(2,1)}, u32[]{:S(2)}, u32[]{:S(2)}) async-start(bf16[32,5,6144]{2,1,0:T(8,128)(2,1)} %bitcast.42), calls=%async_computation | async-start | bytes 6291456 | tf_op jit(solution)/shard_map/all_to_all | solution.py:35
  199.6 148.8 %all-to-all-start.2 = ((bf16[32,5,6144]{2,1,0:T(8,128)(2,1)}), bf16[32,5,6144]{2,1,0:T(8,128)(2,1)}, u32[]{:S(2)}, u32[]{:S(2)}) async-start(bf16[32,5,6144]{2,1,0:T(8,128)(2,1)} %bitcast.43), calls=%async_computation.2 | async-start | bytes 6291456 | tf_op jit(solution)/shard_map/all_to_all | solution.py:36
  204.2 235.4 %reduce-scatter.9.cloned.1.call-start = ((), (), s32[]{:S(2)}) async-start(), calls=%async_computation.7 | async-start | bytes 3342336
  207.3 1.4 copy-start.1
  351.4 2.1 copy-start.3
  351.4 2.1 copy-start.4
  353.5 1.4 copy-start.2
  358.4 175.9 %reduce-scatter.7.cloned.1.call-start = ((), (), s32[]{:S(2)}) async-start(), calls=%async_computation.6 | async-start | bytes 3342336
  363.4 203.9 %copy-start.6 = (f32[16,2]{0,1:T(2,128)S(1)}, f32[16,2]{0,1:T(2,128)}, u32[]{:S(2)}) copy-start(f32[16,2]{0,1:T(2,128)} %param.9) | copy-start | bytes 388
  441.4 94.7 %all-to-all-start.3 = ((bf16[32,5,384]{2,1,0:T(8,128)(2,1)}), bf16[32,5,384]{2,1,0:T(8,128)(2,1)S(1)}, u32[]{:S(2)}, u32[]{:S(2)}) async-start(bf16[32,5,384]{2,1,0:T(8,128)(2,1)} %convert_element_type.142), calls=%async_computation.3 | async-start | bytes 393216 | tf_op jit(solution)/shard_map/all_to_all | solution.py:74
  536.1 31.2 %all-to-all-start.1 = ((bf16[32,5,384]{2,1,0:T(8,128)(2,1)}), bf16[32,5,384]{2,1,0:T(8,128)(2,1)S(1)}, u32[]{:S(2)}, u32[]{:S(2)}) async-start(bf16[32,5,384]{2,1,0:T(8,128)(2,1)} %convert_element_type.134), calls=%async_computation.1 | async-start | bytes 393216 | tf_op jit(solution)/shard_map/all_to_all | solution.py:71
Sparse Core Ops, SparseCore 0:
  358.5 81.0 reduce-scatter.8
  443.8 90.4 reduce-scatter.6
where the time goes:
time: 615 us; the launch traced here: 614 us
  waiting for transfers between devices  433 us (70%)
  blocking collectives  85.8 us (14%)
  starting transfers between devices  45.9 us (7%)
  local copies, waits for them, and re-layouts  21.7 us (4%)
  between operations  14.3 us (2%)
  matrix products  10.8 us (2%)
    unnamed x4, waiting for transfers between devices  156 us
    all_to_all x1, waiting for transfers between devices, per_device(): lax.all_to_all(send_dy, 'expert', split_axis=0, concat_axis=0, tiled=True)  138 us
    all_to_all x1, waiting for transfers between devices, per_device(): lax.all_to_all(send_x, 'expert', split_axis=0, concat_axis=0, tiled=True)  121 us
    psum x1, blocking collectives, per_device(): grad_gates = lax.psum(partial_dots, ('pipe', 'tensor'))  38.7 us
    all_gather x1, blocking collectives, per_device(): lax.all_gather(tokens, ('pipe', 'tensor'), axis=1, tiled=True)  24 us
    all_gather x1, blocking collectives, per_device(): lax.all_gather(d_out, ('pipe', 'tensor'), axis=1, tiled=True)  23.1 us
    all_to_all x1, waiting for transfers between devices, per_device(): lax.all_to_all(out_slot.astype(jnp.bfloat16), 'expert', split_axis=0, con...  17.5 us
    all_to_all x1, starting transfers between devices, per_device(): lax.all_to_all(send_x, 'expert', split_axis=0, concat_axis=0, tiled=True)  15.5 us
  transfers between devices with their start and end apart: 6, of which 5 were waited for; matrix products, arithmetic and copies ran while one was open for 3% of the time, Pallas kernels for 0%

commit v1 on v0

--- a/solution.py
+++ b/solution.py
@@ -24,7 +24,12 @@
     select_tok = jnp.sum(pick_rows, axis=2).astype(jnp.bfloat16)
     select_gate = jnp.sum(pick_rows * gates[None, :, :], axis=2)
     whole_x, whole_dy = (
-        lax.all_gather(tokens, ("pipe", "tensor"), axis=1, tiled=True),
+        jnp.concatenate(
+            lax.all_to_all(
+                jnp.stack([tokens] * lax.axis_size(("pipe", "tensor"))), ("pipe", "tensor"), 0, 0
+            ),
+            axis=1,
+        ),
         lax.all_gather(d_out, ("pipe", "tensor"), axis=1, tiled=True),
     )
     picked = jnp.dot(select_tok, whole_x, preferred_element_type=jnp.float32).astype(jnp.bfloat16)

time: 615 us -> 623 us (1.013)
  waiting for transfers between devices: 433 us -> 457 us
  blocking collectives: 85.8 us -> 62.8 us
  starting transfers between devices: 45.9 us -> 52.7 us
    all_gather x1 -> x0, blocking collectives: 24 us -> none  [per_device(): lax.all_gather(tokens, ('pipe', 'tensor'), axis=1, tiled=True)]
    all_to_all x1, waiting for transfers between devices: 121 us -> 138 us  [per_device(): lax.all_to_all(send_x, 'expert', split_axis=0, concat_axis=0, tiled=True)]
    all_to_all x1, starting transfers between devices: 15.5 us -> 4.61 us  [per_device(): lax.all_to_all(send_x, 'expert', split_axis=0, concat_axis=0, tiled=True)]
    all_to_all x1, starting transfers between devices: 4.6 us -> 15.4 us  [per_device(): lax.all_to_all(send_dy, 'expert', split_axis=0, concat_axis=0, tiled=True)]
    all_to_all x0 -> x1, starting transfers between devices: none -> 7.03 us  [per_device(): lax.all_to_all(jnp.stack([tokens] * lax.axis_size(('pipe', 'tensor'))), (...]
    all_to_all x1, waiting for transfers between devices: 138 us -> 145 us  [per_device(): lax.all_to_all(send_dy, 'expert', split_axis=0, concat_axis=0, tiled=True)]
  transfers between devices with their start and end apart: 6 -> 7, of which waited for: 5 -> 5; matrix products, arithmetic and copies ran while one was open for 3% -> 3% of each run, Pallas kernels for 0% -> 0%
where the time goes in v1:
time: 623 us; the launch traced here: 622 us
  waiting for transfers between devices  457 us (73%)
  blocking collectives  62.8 us (10%)
  starting transfers between devices  52.7 us (8%)
  local copies, waits for them, and re-layouts  23.6 us (4%)
  between operations  14.3 us (2%)
  matrix products  10.2 us (2%)
    unnamed x4, waiting for transfers between devices  156 us
    all_to_all x1, waiting for transfers between devices, per_device(): lax.all_to_all(send_dy, 'expert', split_axis=0, concat_axis=0, tiled=True)  145 us
    all_to_all x1, waiting for transfers between devices, per_device(): lax.all_to_all(send_x, 'expert', split_axis=0, concat_axis=0, tiled=True)  138 us
    psum x1, blocking collectives, per_device(): grad_gates = lax.psum(partial_dots, ('pipe', 'tensor'))  38.7 us
    all_gather x1, blocking collectives, per_device(): lax.all_gather(d_out, ('pipe', 'tensor'), axis=1, tiled=True)  24.1 us
    all_to_all x1, waiting for transfers between devices, per_device(): lax.all_to_all(out_slot.astype(jnp.bfloat16), 'expert', split_axis=0, con...  17.4 us
    all_to_all x1, starting transfers between devices, per_device(): lax.all_to_all(send_dy, 'expert', split_axis=0, concat_axis=0, tiled=True)  15.4 us
    all_to_all x1, starting transfers between devices, per_device(): lax.all_to_all(dx_slot.astype(jnp.bfloat16), 'expert', split_axis=0, conc...  12.8 us
  transfers between devices with their start and end apart: 7, of which 5 were waited for; matrix products, arithmetic and copies ran while one was open for 3% of the time, Pallas kernels for 0%

profile of v1, /device:TPU:32, one launch (start us, length us, event | category | flops | bytes accessed | tf_op | source)
XLA Modules:
  0.0 622.1 jit_solution(15171623242345658910)
XLA Ops:
  7.2 1.5 stack.2
  8.7 7.0 %all-to-all-start = ((bf16[16,16,384]{2,1,0:T(8,128)(2,1)}), bf16[16,16,384]{2,1,0:T(8,128)(2,1)S(1)}, u32[]{:S(2)}, u32[]{:S(2)}) async-start(bf16[16,16,384]{2,1,0:T(8,128)(2,1)} %stack.2), calls=%async_computation | async-start | bytes 393216 | tf_op jit(solution)/shard_map/all_to_all | solution.py:28
  17.8 24.1 %all_gather.3 = bf16[16,6144]{1,0:T(8,128)(2,1)S(1)} all-gather(bf16[16,384]{1,0:T(8,128)(2,1)} %param.13), channel_id=1, replica_groups=mesh['pipe'=4,'expert'=32,'tensor'=4] {'pipe','tensor'}, dimensions={1}, use_global_device_ids=true | all-gather | bytes 208896 | tf_op jit(solution)/shard_map/all_gather | solution.py:33
  43.5 2.0 broadcast_in_dim.5
  45.5 15.4 %all-to-all-start.3 = ((bf16[32,5,6144]{2,1,0:T(8,128)(2,1)}), bf16[32,5,6144]{2,1,0:T(8,128)(2,1)}, u32[]{:S(2)}, u32[]{:S(2)}) async-start(bf16[32,5,6144]{2,1,0:T(8,128)(2,1)} %bitcast.45), calls=%async_computation.3 | async-start | bytes 6291456 | tf_op jit(solution)/shard_map/all_to_all | solution.py:41
  61.5 144.7 %all-to-all-done.3 = bf16[32,5,6144]{2,1,0:T(8,128)(2,1)} async-done(((bf16[32,5,6144]{2,1,0:T(8,128)(2,1)}), bf16[32,5,6144]{2,1,0:T(8,128)(2,1)}, u32[]{:S(2)}, u32[]{:S(2)}) %all-to-all-start.3) | async-done | bytes 1966112 | tf_op jit(solution)/shard_map/all_to_all | solution.py:41
  206.2 2.1 broadcast_in_dim.4
  208.2 4.6 all-to-all-start.1
  212.9 3.0 reshape.145
  215.9 2.7 fusion.1
  218.6 138.4 %all-to-all-done.1 = bf16[32,5,6144]{2,1,0:T(8,128)(2,1)} async-done(((bf16[32,5,6144]{2,1,0:T(8,128)(2,1)}), bf16[32,5,6144]{2,1,0:T(8,128)(2,1)}, u32[]{:S(2)}, u32[]{:S(2)}) %all-to-all-start.1) | async-done | bytes 1966112 | tf_op jit(solution)/shard_map/all_to_all | solution.py:40
  357.0 3.0 reshape.140
  364.2 2.8 copy.37
  367.0 2.2 convolution_convert_fusion
  369.2 2.8 copy.35
  372.0 76.1 %reduce-scatter.9.cloned.1.call-done = bf16[384,160]{1,0:T(8,128)(2,1)} async-done(((bf16[6144,160]{1,0:T(8,128)(2,1)}), bf16[384,160]{1,0:T(8,128)(2,1)}) %reduce-scatter.9.cloned.1.call-update) | async-done | bytes 122896
  448.0 1.1 copy.38
  449.8 12.8 %all-to-all-start.4 = ((bf16[32,5,384]{2,1,0:T(8,128)(2,1)}), bf16[32,5,384]{2,1,0:T(8,128)(2,1)S(1)}, u32[]{:S(2)}, u32[]{:S(2)}) async-start(bf16[32,5,384]{2,1,0:T(8,128)(2,1)} %convert_element_type.142), calls=%async_computation.4 | async-start | bytes 393216 | tf_op jit(solution)/shard_map/all_to_all | solution.py:79
  462.6 80.0 %reduce-scatter.7.cloned.1.call-done = bf16[384,160]{1,0:T(8,128)(2,1)} async-done(((bf16[6144,160]{1,0:T(8,128)(2,1)}), bf16[384,160]{1,0:T(8,128)(2,1)}) %reduce-scatter.7.cloned.1.call-update) | async-done | bytes 122896
  542.7 1.1 copy.36
  544.5 12.8 %all-to-all-start.2 = ((bf16[32,5,384]{2,1,0:T(8,128)(2,1)}), bf16[32,5,384]{2,1,0:T(8,128)(2,1)S(1)}, u32[]{:S(2)}, u32[]{:S(2)}) async-start(bf16[32,5,384]{2,1,0:T(8,128)(2,1)} %convert_element_type.134), calls=%async_computation.2 | async-start | bytes 393216 | tf_op jit(solution)/shard_map/all_to_all | solution.py:76
  558.2 17.4 %all-to-all-done.2 = bf16[32,5,384]{2,1,0:T(8,128)(2,1)S(1)} async-done(((bf16[32,5,384]{2,1,0:T(8,128)(2,1)}), bf16[32,5,384]{2,1,0:T(8,128)(2,1)S(1)}, u32[]{:S(2)}, u32[]{:S(2)}) %all-to-all-start.2) | async-done | bytes 122912 | tf_op jit(solution)/shard_map/all_to_all | solution.py:76
  575.7 0.9 multiply_reduce_fusion
  576.6 38.7 %psum.7 = f32[16,2]{0,1:T(2,128)} all-reduce(f32[16,2]{0,1:T(2,128)S(1)} %get-tuple-element.3), channel_id=1, replica_groups=mesh['pipe'=4,'expert'=32,'tensor'=4] {'pipe','tensor'}, use_global_device_ids=true, to_apply=%region_11.12 | all-reduce | flops 32 | bytes 256 | tf_op jit(solution)/shard_map/psum | solution.py:101
  (47 shorter events, 10.7 us)
Async XLA Ops:
  7.2 352.9 %copy-start = (bf16[1,6144,128]{2,1,0:T(8,128)(2,1)S(1)}, bf16[1,6144,128]{2,1,0:T(8,128)(2,1)}, u32[]{:S(2)}) copy-start(bf16[1,6144,128]{2,1,0:T(8,128)(2,1)} %param.10) | copy-start | bytes 4718596
  8.7 34.8 %all-to-all-start = ((bf16[16,16,384]{2,1,0:T(8,128)(2,1)}), bf16[16,16,384]{2,1,0:T(8,128)(2,1)S(1)}, u32[]{:S(2)}, u32[]{:S(2)}) async-start(bf16[16,16,384]{2,1,0:T(8,128)(2,1)} %stack.2), calls=%async_computation | async-start | bytes 393216 | tf_op jit(solution)/shard_map/all_to_all | solution.py:28
  45.5 160.7 %all-to-all-start.3 = ((bf16[32,5,6144]{2,1,0:T(8,128)(2,1)}), bf16[32,5,6144]{2,1,0:T(8,128)(2,1)}, u32[]{:S(2)}, u32[]{:S(2)}) async-start(bf16[32,5,6144]{2,1,0:T(8,128)(2,1)} %bitcast.45), calls=%async_computation.3 | async-start | bytes 6291456 | tf_op jit(solution)/shard_map/all_to_all | solution.py:41
  208.2 148.8 %all-to-all-start.1 = ((bf16[32,5,6144]{2,1,0:T(8,128)(2,1)}), bf16[32,5,6144]{2,1,0:T(8,128)(2,1)}, u32[]{:S(2)}, u32[]{:S(2)}) async-start(bf16[32,5,6144]{2,1,0:T(8,128)(2,1)} %bitcast.46), calls=%async_computation.1 | async-start | bytes 6291456 | tf_op jit(solution)/shard_map/all_to_all | solution.py:40
  212.8 235.2 %reduce-scatter.9.cloned.1.call-start = ((), (), s32[]{:S(2)}) async-start(), calls=%async_computation.8 | async-start | bytes 3342336
  360.0 1.4 copy-start.1
  361.4 2.0 copy-start.2
  361.4 1.3 copy-start.4
  362.1 0.6 copy-start.3
  366.9 175.7 %reduce-scatter.7.cloned.1.call-start = ((), (), s32[]{:S(2)}) async-start(), calls=%async_computation.7 | async-start | bytes 3342336
  371.9 185.3 %copy-start.5 = (bf16[16,384]{1,0:T(8,128)(2,1)S(1)}, bf16[16,384]{1,0:T(8,128)(2,1)}, u32[]{:S(2)}) copy-start(bf16[16,384]{1,0:T(8,128)(2,1)} %param.13) | copy-start | bytes 36868
  372.0 203.7 %copy-start.6 = (f32[16,2]{0,1:T(2,128)S(1)}, f32[16,2]{0,1:T(2,128)}, u32[]{:S(2)}) copy-start(f32[16,2]{0,1:T(2,128)} %param.9) | copy-start | bytes 388
  449.8 94.6 %all-to-all-start.4 = ((bf16[32,5,384]{2,1,0:T(8,128)(2,1)}), bf16[32,5,384]{2,1,0:T(8,128)(2,1)S(1)}, u32[]{:S(2)}, u32[]{:S(2)}) async-start(bf16[32,5,384]{2,1,0:T(8,128)(2,1)} %convert_element_type.142), calls=%async_computation.4 | async-start | bytes 393216 | tf_op jit(solution)/shard_map/all_to_all | solution.py:79
  544.5 31.1 %all-to-all-start.2 = ((bf16[32,5,384]{2,1,0:T(8,128)(2,1)}), bf16[32,5,384]{2,1,0:T(8,128)(2,1)S(1)}, u32[]{:S(2)}, u32[]{:S(2)}) async-start(bf16[32,5,384]{2,1,0:T(8,128)(2,1)} %convert_element_type.134), calls=%async_computation.2 | async-start | bytes 393216 | tf_op jit(solution)/shard_map/all_to_all | solution.py:76
Sparse Core Ops, SparseCore 0:
  367.1 80.9 reduce-scatter.8
  452.2 90.3 reduce-scatter.6
